TPU v7x, 32 devices: a whole 2x2x4 slice. The times are simulated.
32 devices in a mesh: gx: 4 (over z), gy: 2 (over y), gz: 4 (over x, core).
Axes of the slice: x: 2, y: 2, z: 4, core: 2. Of those that a mesh axis runs over, the one named last changes fastest.
Arguments:
- positions: float32 [3, 4, 2, 8, 128], P(None, 'gx', 'gy', 'gz'), may hold values from 0 to 8, as said below
- velocity: float32 [3, 4, 2, 8, 128], P(None, 'gx', 'gy', 'gz'), may hold values from -16 to 16
- counts: int32 [4, 2, 8], P('gx', 'gy', 'gz'), may hold values from 0 to 128, as said below
Outputs:
- velocity_new: float32 [3, 4, 2, 8, 128], P(None, 'gx', 'gy', 'gz')
- pressure: float32 [4, 2, 8, 128], P('gx', 'gy', 'gz')
Inputs may be any that keep to these rules, and one draw needn't show every extreme that they name: `positions`: component k of the position of any slot of tile (a, b, c) lies in [t, t + 1), where t is a, b or c for k = 0, 1, 2. A tile's particles fill its first counts[a, b, c] slots. In every column of tiles the bottom tile is full, the tiles below one topmost wet tile hold 96 or more particles, and the tiles above it are empty.
All inputs are finite; a program needn't handle non-finite values.
Results may differ from a plain program's by a relative error of at most 0.0003.
Values sent between devices are 32-bit elements; how exact they have to be, the bound alone decides.
No kernel may reach another device: no remote copies, remote signals or barrier semaphores. Data moves between devices by JAX's collectives and lax.ppermute only.
A program may use at most 64 MiB of HBM per device.

v0:
```python
import jax
import jax.numpy as jnp
from jax import lax
from jax.sharding import PartitionSpec as P

ITERS = 3
DIAG_SHIFT = 0.05
VISCOSITY = 0.5
GRAVITY = 0.1
GRADIENT_GAIN = 32.0
AXES = (("gx", 1), ("gy", 2), ("gz", 3))


def with_halo(cells, sides, width):
    for axis, dim in sides:
        count = lax.axis_size(axis)
        ends = count - 1
        head = lax.slice_in_dim(cells, 0, width, axis=dim)
        tail = lax.slice_in_dim(cells, cells.shape[dim] - width, cells.shape[dim], axis=dim)
        cells = jnp.concatenate(
            [
                lax.ppermute(tail, axis, [(i, (i + 1) % count) for i in range(ends)]),
                cells,
                lax.ppermute(head, axis, [((i + 1) % count, i) for i in range(ends)]),
            ],
            axis=dim,
        )
    return cells


def neighbours(rim):
    comps, size_x, size_y, size_z, width = rim.shape
    blocks = []
    for ax in range(size_x - 2):
        for ay in range(size_y - 2):
            for az in range(size_z - 2):
                window = rim[:, ax : ax + 3, ay : ay + 3, az : az + 3, :]
                blocks.append(window.reshape(comps, 27 * width))
    return jnp.stack(blocks, axis=1)


def flat(cells):
    return cells.reshape(cells.shape[0], -1, cells.shape[4])


def wsum(weight, near):
    return jnp.sum(weight[None] * near[:, :, None, :], axis=-1)


def tile_corners(block_shape):
    _, size_x, size_y, size_z, _ = block_shape
    base = (
        lax.axis_index("gx") * size_x,
        lax.axis_index("gy") * size_y,
        lax.axis_index("gz") * size_z,
    )
    corners = []
    for ax in range(size_x):
        for ay in range(size_y):
            for az in range(size_z):
                corners.append(jnp.stack([base[0] + ax, base[1] + ay, base[2] + az]))
    return jnp.stack(corners, axis=1).astype(jnp.float32)


def on_device(positions, velocity, counts):
    block_shape = positions.shape
    width = positions.shape[4]
    slot_ids = jnp.arange(width, dtype=jnp.int32)
    valid_mask = (slot_ids[None, None, None, :] < counts[:, :, :, None]).astype(jnp.float32)[None]
    packed = jnp.concatenate([positions, valid_mask, velocity], axis=0)
    near_all = neighbours(with_halo(packed, AXES, 1))
    near_x = near_all[0:3]
    near_valid = near_all[3]
    near_v = near_all[4:7]
    own_x = flat(positions)
    own_valid = flat(valid_mask)[0]
    own_v = flat(velocity)
    offset = own_x[:, :, :, None] - near_x[:, :, None, :]
    distance = offset[0] * offset[0] + offset[1] * offset[1] + offset[2] * offset[2]
    closeness = jnp.maximum(1.0 - distance, 0.0)
    weight = closeness * closeness * own_valid[:, :, None] * near_valid[:, None, :]
    corner = tile_corners(block_shape)[:, :, None]
    local_own = own_x - corner
    local_near = near_x - corner
    row = jnp.sum(weight, axis=-1)[None]
    sums = wsum(weight, jnp.concatenate([near_v, local_near], axis=0))
    near_sums = sums[0:3]
    lever = local_own * row - sums[3:6]
    gravity_pull = jnp.array([0.0, 0.0, -GRAVITY], jnp.float32).reshape(3, 1, 1)
    predicted = own_valid[None] * (
        own_v + VISCOSITY / width * (near_sums - row * own_v) + gravity_pull
    )
    diagonal = DIAG_SHIFT + row / width

    def shaped(values):
        return values.reshape(values.shape[0], *block_shape[1:])

    near_pred = neighbours(with_halo(shaped(predicted), AXES, 1))
    dotted = jnp.sum(near_pred * local_near, axis=0, keepdims=True)
    psums = wsum(weight, jnp.concatenate([near_pred, dotted], axis=0))
    flux = jnp.sum(local_own * psums[0:3], axis=0, keepdims=True) - psums[3:4]
    source = -(GRADIENT_GAIN / width) * (jnp.sum(predicted * lever, axis=0, keepdims=True) - flux)

    def operate(field):
        near_field = neighbours(with_halo(shaped(field), AXES, 1))
        return (near_field, diagonal * field - wsum(weight, near_field) / width)

    def paired_sums(residual, precond, applied):
        pair = jnp.stack([jnp.sum(residual * precond), jnp.sum(precond * applied)])
        total = lax.psum(pair, ("gx", "gy", "gz"))
        return (total[0], total[1])

    pressure = jnp.zeros_like(source)
    residual = source
    precond = residual / diagonal
    near_dir, applied = operate(precond)
    norm_now, curvature_sum = paired_sums(residual, precond, applied)
    step_size = norm_now / curvature_sum
    direction = precond
    along = applied
    near_pressure = jnp.zeros_like(near_dir)
    for iteration in range(ITERS):
        pressure = pressure + step_size * direction
        near_pressure = near_pressure + step_size * near_dir
        residual = residual - step_size * along
        if iteration + 1 < ITERS:
            precond = residual / diagonal
            near_fresh, applied = operate(precond)
            norm_next, curvature_sum = paired_sums(residual, precond, applied)
            blend = norm_next / norm_now
            step_size = norm_next / (curvature_sum - blend * norm_next / step_size)
            direction = precond + blend * direction
            near_dir = near_fresh + blend * near_dir
            along = applied + blend * along
            norm_now = norm_next
    grads = wsum(weight, jnp.concatenate([near_pressure, near_pressure * local_near], axis=0))
    moments = local_own * grads[0:1] - grads[1:4]
    velocity_new = predicted - GRADIENT_GAIN / width * (pressure * lever - moments)
    return (shaped(velocity_new), shaped(pressure)[0])


def solution(mesh):
    in_specs = (
        P(None, "gx", "gy", "gz", None),
        P(None, "gx", "gy", "gz", None),
        P("gx", "gy", "gz"),
    )
    out_specs = (P(None, "gx", "gy", "gz", None), P("gx", "gy", "gz", None))
    return jax.shard_map(
        on_device, mesh=mesh, in_specs=in_specs, out_specs=out_specs, check_vma=False
    )
```

profile of v0, /device:TPU:0, one launch (start us, length us, event | category | flops | bytes accessed | tf_op | source)
XLA Modules:
  0.0 319.3 jit_solution(7614055411883678423)
XLA Ops:
  2.7 1.3 collective-permute-start.1
  4.0 5.6 %collective-permute-start = (f32[7,1,1,2,128]{4,0,3,2,1:T(8,128)S(1)}, f32[7,1,1,2,128]{4,0,3,2,1:T(8,128)S(1)}, u32[]{:S(2)}, u32[]{:S(2)}) collective-permute-start(f32[7,1,1,2,128]{4,0,3,2,1:T(8,128)S(1)} %pad_maximum_fusion.19), channel_id=1, source_target_pairs={{0,8},{8,16},{16,24},{1,9},{9,17},{17,25},{2,10},{10,18},{18,26},{... | collective-permute-start | bytes 21512 | tf_op jit(solution)/shard_map/ppermute | solution.py:22
  12.3 4.5 %collective-permute-start.2 = (f32[7,3,1,2,128]{4,0,3,2,1:T(8,128)S(1)}, f32[7,3,1,2,128]{4,0,3,2,1:T(8,128)S(1)}, u32[]{:S(2)}, u32[]{:S(2)}) collective-permute-start(f32[7,3,1,2,128]{4,0,3,2,1:T(8,128)S(1)} %pad_maximum_fusion.11), channel_id=1, source_target_pairs={{0,4},{1,5},{2,6},{3,7},{8,12},{9,13},{10,14},{11,15},{16,20},{17,... | collective-permute-start | bytes 64520 | tf_op jit(solution)/shard_map/ppermute | solution.py:22
  16.9 1.4 collective-permute-done.2
  18.3 1.3 collective-permute-start.4
  19.6 1.3 collective-permute-start.5
  21.0 3.9 %collective-permute-done.5 = f32[7,3,3,1,128]{4,0,3,2,1:T(8,128)S(1)} collective-permute-done((f32[7,3,3,1,128]{4,0,3,2,1:T(8,128)S(1)}, f32[7,3,3,1,128]{4,0,3,2,1:T(8,128)S(1)}, u32[]{:S(2)}, u32[]{:S(2)}) %collective-permute-start.5) | collective-permute-done | bytes 32288 | tf_op jit(solution)/shard_map/ppermute | solution.py:24
  25.7 1.5 broadcast_subtract_fusion
  27.2 1.6 fusion.6
  29.3 1.7 copy-done
  31.0 1.8 multiply_reduce_fusion
  34.2 4.8 %collective-permute-start.6 = (f32[3,1,1,2,128]{4,3,0,2,1:T(2,128)S(1)}, f32[3,1,1,2,128]{4,3,0,2,1:T(2,128)S(1)}, u32[]{:S(2)}, u32[]{:S(2)}) collective-permute-start(f32[3,1,1,2,128]{4,3,0,2,1:T(2,128)S(1)} %bitcast.144), channel_id=1, source_target_pairs={{0,8},{8,16},{16,24},{1,9},{9,17},{17,25},{2,10},{10,18},{18,26},{... | collective-permute-start | bytes 9224 | tf_op jit(solution)/shard_map/ppermute | solution.py:22
  39.1 1.3 collective-permute-done.6
  40.4 1.3 collective-permute-start.9
  41.7 4.5 %collective-permute-start.8 = (f32[3,3,1,2,128]{4,3,0,2,1:T(2,128)S(1)}, f32[3,3,1,2,128]{4,3,0,2,1:T(2,128)S(1)}, u32[]{:S(2)}, u32[]{:S(2)}) collective-permute-start(f32[3,3,1,2,128]{4,3,0,2,1:T(2,128)S(1)} %pad_maximum_fusion.15), channel_id=1, source_target_pairs={{0,4},{1,5},{2,6},{3,7},{8,12},{9,13},{10,14},{11,15},{16,20},{17,... | collective-permute-start | bytes 27656 | tf_op jit(solution)/shard_map/ppermute | solution.py:22
  46.2 1.3 collective-permute-done.8
  49.5 3.8 %collective-permute-start.10 = (f32[3,3,3,1,128]{4,3,0,2,1:T(1,128)}, f32[3,3,3,1,128]{4,3,0,2,1:T(1,128)}, u32[]{:S(2)}, u32[]{:S(2)}) collective-permute-start(f32[3,3,3,1,128]{4,3,0,2,1:T(1,128)} %get-tuple-element.28), channel_id=1, source_target_pairs={{0,1},{1,2},{2,3},{4,5},{5,6},{6,7},{8,9},{9,10},{10,11},{12,13},{... | collective-permute-start | bytes 41480 | tf_op jit(solution)/shard_map/ppermute | solution.py:22
  53.4 1.3 copy.31
  54.7 1.5 pad_maximum_fusion.5
  56.8 1.5 stack_reshape.32
  58.3 1.4 constant_dynamic-update-slice_fusion.1
  59.7 1.4 copy.33
  61.1 1.5 stack_reshape.33
  62.6 1.4 constant_dynamic-update-slice_fusion
  66.1 3.3 %multiply_reduce_fusion.2 = f32[4,2,128]{2,1,0:T(2,128)S(1)} fusion(f32[4,2,3456]{2,1,0:T(2,128)S(1)} %copy.34, f32[2,128,3456]{2,1,0:T(8,128)} %copy-done), kind=kLoop, calls=%fused_computation.2 | loop fusion | flops 7076864 | bytes 3653632 | tf_op jit(solution)/shard_map/reduce_sum | solution.py:47
  71.4 4.6 %collective-permute-start.12 = (f32[1,1,1,2,128]{4,3,2,1,0:T(2,128)S(1)}, f32[1,1,1,2,128]{4,3,2,1,0:T(2,128)S(1)}, u32[]{:S(2)}, u32[]{:S(2)}) collective-permute-start(f32[1,1,1,2,128]{4,3,2,1,0:T(2,128)S(1)} %bitcast.160), channel_id=1, source_target_pairs={{0,8},{8,16},{16,24},{1,9},{9,17},{17,25},{2,10},{10,18},{18,26},{... | collective-permute-start | bytes 3080 | tf_op jit(solution)/shard_map/ppermute | solution.py:22
  78.6 4.5 %collective-permute-start.14 = (f32[1,3,1,2,128]{4,3,2,1,0:T(2,128)S(1)}, f32[1,3,1,2,128]{4,3,2,1,0:T(2,128)S(1)}, u32[]{:S(2)}, u32[]{:S(2)}) collective-permute-start(f32[1,3,1,2,128]{4,3,2,1,0:T(2,128)S(1)} %pad_maximum_fusion.20), channel_id=1, source_target_pairs={{0,4},{1,5},{2,6},{3,7},{8,12},{9,13},{10,14},{11,15},{16,20},{17,... | collective-permute-start | bytes 9224 | tf_op jit(solution)/shard_map/ppermute | solution.py:22
  83.2 1.3 collective-permute-done.14
  84.5 1.5 collective-permute-start.16
  86.0 1.3 collective-permute-start.17
  87.3 5.3 %collective-permute-done.17 = f32[1,3,3,1,128]{4,3,2,1,0:T(1,128)S(1)} collective-permute-done((f32[1,3,3,1,128]{4,3,2,1,0:T(1,128)S(1)}, f32[1,3,3,1,128]{4,3,2,1,0:T(1,128)S(1)}, u32[]{:S(2)}, u32[]{:S(2)}) %collective-permute-start.17) | collective-permute-done | bytes 4640 | tf_op jit(solution)/shard_map/ppermute | solution.py:24
  94.0 1.3 stack_reshape.34
  96.1 1.4 multiply_reduce_fusion.5
  98.8 1.8 pad_maximum_fusion.23
  100.6 43.4 %psum.21 = f32[2]{0:T(128)} all-reduce(f32[2]{0:T(128)} %pad_maximum_fusion.23), channel_id=1, replica_groups=mesh['gx'=4,'gy'=2,'gz'=4] {'gx','gy','gz'}, use_global_device_ids=true, to_apply=%region_9.0 | all-reduce | flops 2 | bytes 16 | tf_op jit(solution)/shard_map/psum | solution.py:110
  144.0 1.3 fusion.36
  148.7 4.5 %collective-permute-start.18 = (f32[1,1,1,2,128]{4,3,2,1,0:T(2,128)S(1)}, f32[1,1,1,2,128]{4,3,2,1,0:T(2,128)S(1)}, u32[]{:S(2)}, u32[]{:S(2)}) collective-permute-start(f32[1,1,1,2,128]{4,3,2,1,0:T(2,128)S(1)} %bitcast.149), channel_id=1, source_target_pairs={{0,8},{8,16},{16,24},{1,9},{9,17},{17,25},{2,10},{10,18},{18,26},{... | collective-permute-start | bytes 3080 | tf_op jit(solution)/shard_map/ppermute | solution.py:22
  155.9 4.5 %collective-permute-start.20 = (f32[1,3,1,2,128]{4,3,2,1,0:T(2,128)S(1)}, f32[1,3,1,2,128]{4,3,2,1,0:T(2,128)S(1)}, u32[]{:S(2)}, u32[]{:S(2)}) collective-permute-start(f32[1,3,1,2,128]{4,3,2,1,0:T(2,128)S(1)} %pad_maximum_fusion.21), channel_id=1, source_target_pairs={{0,4},{1,5},{2,6},{3,7},{8,12},{9,13},{10,14},{11,15},{16,20},{17,... | collective-permute-start | bytes 9224 | tf_op jit(solution)/shard_map/ppermute | solution.py:22
  160.4 1.3 collective-permute-done.20
  161.7 1.3 collective-permute-start.22
  163.0 1.3 collective-permute-start.23
  164.4 4.3 %collective-permute-done.23 = f32[1,3,3,1,128]{4,3,2,1,0:T(1,128)S(1)} collective-permute-done((f32[1,3,3,1,128]{4,3,2,1,0:T(1,128)S(1)}, f32[1,3,3,1,128]{4,3,2,1,0:T(1,128)S(1)}, u32[]{:S(2)}, u32[]{:S(2)}) %collective-permute-start.23) | collective-permute-done | bytes 4640 | tf_op jit(solution)/shard_map/ppermute | solution.py:24
  169.2 1.3 stack_reshape.37
  170.6 1.3 stack_reshape.36
  172.7 1.4 multiply_reduce_fusion.4
  174.2 1.4 multiply_reduce_fusion.10
  175.5 1.8 pad_maximum_fusion.24
  177.4 43.4 %psum.22 = f32[2]{0:T(128)} all-reduce(f32[2]{0:T(128)} %pad_maximum_fusion.24), channel_id=1, replica_groups=mesh['gx'=4,'gy'=2,'gz'=4] {'gx','gy','gz'}, use_global_device_ids=true, to_apply=%region_13.0 | all-reduce | flops 2 | bytes 16 | tf_op jit(solution)/shard_map/psum | solution.py:110
  220.7 1.3 fusion.35
  229.1 4.5 %collective-permute-start.24 = (f32[1,1,1,2,128]{4,3,2,1,0:T(2,128)S(1)}, f32[1,1,1,2,128]{4,3,2,1,0:T(2,128)S(1)}, u32[]{:S(2)}, u32[]{:S(2)}) collective-permute-start(f32[1,1,1,2,128]{4,3,2,1,0:T(2,128)S(1)} %bitcast.155), channel_id=1, source_target_pairs={{0,8},{8,16},{16,24},{1,9},{9,17},{17,25},{2,10},{10,18},{18,26},{... | collective-permute-start | bytes 3080 | tf_op jit(solution)/shard_map/ppermute | solution.py:22
  236.3 4.5 %collective-permute-start.26 = (f32[1,3,1,2,128]{4,3,2,1,0:T(2,128)S(1)}, f32[1,3,1,2,128]{4,3,2,1,0:T(2,128)S(1)}, u32[]{:S(2)}, u32[]{:S(2)}) collective-permute-start(f32[1,3,1,2,128]{4,3,2,1,0:T(2,128)S(1)} %pad_maximum_fusion.22), channel_id=1, source_target_pairs={{0,4},{1,5},{2,6},{3,7},{8,12},{9,13},{10,14},{11,15},{16,20},{17,... | collective-permute-start | bytes 9224 | tf_op jit(solution)/shard_map/ppermute | solution.py:22
  242.7 1.9 collective-permute-start.28
  244.6 1.5 collective-permute-start.29
  246.1 1.3 stack.113
  247.4 1.3 stack.112
  248.8 1.3 stack.116
  250.1 1.3 stack.115
  251.5 1.4 maximum_maximum_fusion.4
  252.9 1.3 stack.119
  254.2 1.3 stack_reshape.39
  255.5 1.3 stack_reshape.38
  257.7 1.4 multiply_reduce_fusion.3
  262.5 45.0 %psum.23 = f32[2]{0:T(128)S(1)} all-reduce(f32[2]{0:T(128)S(1)} %pad_maximum_fusion.25), channel_id=1, replica_groups=mesh['gx'=4,'gy'=2,'gz'=4] {'gx','gy','gz'}, use_global_device_ids=true, to_apply=%region_17.0 | all-reduce | flops 2 | bytes 16 | tf_op jit(solution)/shard_map/psum | solution.py:110
  315.3 3.3 %multiply_reduce_fusion.1 = f32[4,2,128]{2,1,0:T(2,128)S(1)} fusion(f32[4,2,3456]{2,1,0:T(2,128)S(1)} %copy.41, f32[2,128,3456]{2,1,0:T(8,128)} %copy-done), kind=kLoop, calls=%fused_computation.1 | loop fusion | flops 7076864 | bytes 3653632 | tf_op jit(solution)/shard_map/reduce_sum | solution.py:47
  (166 shorter events, 41.7 us)
Async XLA Ops:
  2.7 7.6 %collective-permute-start.1 = (f32[7,1,1,2,128]{4,0,3,2,1:T(8,128)S(1)}, f32[7,1,1,2,128]{4,0,3,2,1:T(8,128)S(1)}, u32[]{:S(2)}, u32[]{:S(2)}) collective-permute-start(f32[7,1,1,2,128]{4,0,3,2,1:T(8,128)S(1)} %pad_maximum_fusion.19), channel_id=1, source_target_pairs={{8,0},{16,8},{24,16},{9,1},{17,9},{25,17},{10,2},{18,10},{26,18},{... | collective-permute-start | bytes 21512 | tf_op jit(solution)/shard_map/ppermute | solution.py:24
  4.0 6.9 %collective-permute-start = (f32[7,1,1,2,128]{4,0,3,2,1:T(8,128)S(1)}, f32[7,1,1,2,128]{4,0,3,2,1:T(8,128)S(1)}, u32[]{:S(2)}, u32[]{:S(2)}) collective-permute-start(f32[7,1,1,2,128]{4,0,3,2,1:T(8,128)S(1)} %pad_maximum_fusion.19), channel_id=1, source_target_pairs={{0,8},{8,16},{16,24},{1,9},{9,17},{17,25},{2,10},{10,18},{18,26},{... | collective-permute-start | bytes 21512 | tf_op jit(solution)/shard_map/ppermute | solution.py:22
  10.3 22.5 %copy-start.21 = (f32[2,128]{1,0:T(2,128)}, f32[2,128]{1,0:T(2,128)S(1)}, u32[]{:S(2)}) copy-start(f32[2,128]{1,0:T(2,128)S(1)} %compare_convert_fusion.1) | copy-start | bytes 3076
  11.0 5.9 %collective-permute-start.3 = (f32[7,3,1,2,128]{4,0,3,2,1:T(8,128)S(1)}, f32[7,3,1,2,128]{4,0,3,2,1:T(8,128)S(1)}, u32[]{:S(2)}, u32[]{:S(2)}) collective-permute-start(f32[7,3,1,2,128]{4,0,3,2,1:T(8,128)S(1)} %pad_maximum_fusion.11), channel_id=1, source_target_pairs={{4,0},{5,1},{6,2},{7,3},{12,8},{13,9},{14,10},{15,11},{20,16},{21,... | collective-permute-start | bytes 64520 | tf_op jit(solution)/shard_map/ppermute | solution.py:24
  12.3 6.1 %collective-permute-start.2 = (f32[7,3,1,2,128]{4,0,3,2,1:T(8,128)S(1)}, f32[7,3,1,2,128]{4,0,3,2,1:T(8,128)S(1)}, u32[]{:S(2)}, u32[]{:S(2)}) collective-permute-start(f32[7,3,1,2,128]{4,0,3,2,1:T(8,128)S(1)} %pad_maximum_fusion.11), channel_id=1, source_target_pairs={{0,4},{1,5},{2,6},{3,7},{8,12},{9,13},{10,14},{11,15},{16,20},{17,... | collective-permute-start | bytes 64520 | tf_op jit(solution)/shard_map/ppermute | solution.py:22
  18.3 2.6 collective-permute-start.4
  19.6 5.3 %collective-permute-start.5 = (f32[7,3,3,1,128]{4,0,3,2,1:T(8,128)S(1)}, f32[7,3,3,1,128]{4,0,3,2,1:T(8,128)S(1)}, u32[]{:S(2)}, u32[]{:S(2)}) collective-permute-start(f32[7,3,3,1,128]{4,0,3,2,1:T(8,128)S(1)} %get-tuple-element.24), channel_id=1, source_target_pairs={{1,0},{2,1},{3,2},{5,4},{6,5},{7,6},{9,8},{10,9},{11,10},{13,12},{... | collective-permute-start | bytes 96776 | tf_op jit(solution)/shard_map/ppermute | solution.py:24
  21.0 6.3 %copy-start.30 = (f32[3,2]{0,1:T(2,128)}, f32[3,2]{0,1:T(2,128)S(1)}, u32[]{:S(2)}) copy-start(f32[3,2]{0,1:T(2,128)S(1)} %add_convert_fusion) | copy-start | bytes 76
  25.3 3.6 %copy-start.2 = (f32[1,2,3456]{2,1,0:T(2,128)}, f32[1,2,3456]{2,1,0:T(2,128)S(1)}, u32[]{:S(2)}) copy-start(f32[1,2,3456]{2,1,0:T(2,128)S(1)} %copy.54) | copy-start | bytes 82948
  28.9 40.6 %copy-start.5 = (f32[2,128]{1,0:T(2,128)}, f32[2,128]{1,0:T(2,128)S(1)}, u32[]{:S(2)}) copy-start(f32[2,128]{1,0:T(2,128)S(1)} %get-tuple-element.17) | copy-start | bytes 3076
  29.3 1.7 copy-start
  31.0 1.8 copy-start.29
  31.0 1.8 copy-start.36
  32.8 15.4 %copy-start.12 = (f32[6,2,128]{2,1,0:T(2,128)}, f32[6,2,128]{2,1,0:T(2,128)S(1)}, u32[]{:S(2)}) copy-start(f32[6,2,128]{2,1,0:T(2,128)S(1)} %multiply_reduce_fusion) | copy-start | bytes 18436
  32.8 36.6 %copy-start.10 = (f32[3,1,1,2,128]{4,3,2,1,0:T(2,128)S(1)}, f32[3,1,1,2,128]{4,3,2,1,0:T(2,128)}, u32[]{:S(2)}) copy-start(f32[3,1,1,2,128]{4,3,2,1,0:T(2,128)} %param.4) | copy-start | bytes 9220
  32.9 60.3 %copy-start.3 = (f32[3,2,128]{2,1,0:T(2,128)}, f32[3,2,128]{2,1,0:T(2,128)S(1)}, u32[]{:S(2)}) copy-start(f32[3,2,128]{2,1,0:T(2,128)S(1)} %fusion.20) | copy-start | bytes 9220
  32.9 6.1 %collective-permute-start.7 = (f32[3,1,1,2,128]{4,3,0,2,1:T(2,128)S(1)}, f32[3,1,1,2,128]{4,3,0,2,1:T(2,128)S(1)}, u32[]{:S(2)}, u32[]{:S(2)}) collective-permute-start(f32[3,1,1,2,128]{4,3,0,2,1:T(2,128)S(1)} %bitcast.143), channel_id=1, source_target_pairs={{8,0},{16,8},{24,16},{9,1},{17,9},{25,17},{10,2},{18,10},{26,18},{... | collective-permute-start | bytes 9224 | tf_op jit(solution)/shard_map/ppermute | solution.py:24
  34.2 6.1 %collective-permute-start.6 = (f32[3,1,1,2,128]{4,3,0,2,1:T(2,128)S(1)}, f32[3,1,1,2,128]{4,3,0,2,1:T(2,128)S(1)}, u32[]{:S(2)}, u32[]{:S(2)}) collective-permute-start(f32[3,1,1,2,128]{4,3,0,2,1:T(2,128)S(1)} %bitcast.144), channel_id=1, source_target_pairs={{0,8},{8,16},{16,24},{1,9},{9,17},{17,25},{2,10},{10,18},{18,26},{... | collective-permute-start | bytes 9224 | tf_op jit(solution)/shard_map/ppermute | solution.py:22
  40.4 9.2 %copy-start.22 = (f32[3,1,1,2,128]{4,3,0,2,1:T(2,128)}, f32[3,1,1,2,128]{4,3,0,2,1:T(2,128)S(1)}, u32[]{:S(2)}) copy-start(f32[3,1,1,2,128]{4,3,0,2,1:T(2,128)S(1)} %collective-permute-done.6) | copy-start | bytes 9220
  40.4 5.9 %collective-permute-start.9 = (f32[3,3,1,2,128]{4,3,0,2,1:T(2,128)S(1)}, f32[3,3,1,2,128]{4,3,0,2,1:T(2,128)S(1)}, u32[]{:S(2)}, u32[]{:S(2)}) collective-permute-start(f32[3,3,1,2,128]{4,3,0,2,1:T(2,128)S(1)} %pad_maximum_fusion.15), channel_id=1, source_target_pairs={{4,0},{5,1},{6,2},{7,3},{12,8},{13,9},{14,10},{15,11},{20,16},{21,... | collective-permute-start | bytes 27656 | tf_op jit(solution)/shard_map/ppermute | solution.py:24
  41.7 5.9 %collective-permute-start.8 = (f32[3,3,1,2,128]{4,3,0,2,1:T(2,128)S(1)}, f32[3,3,1,2,128]{4,3,0,2,1:T(2,128)S(1)}, u32[]{:S(2)}, u32[]{:S(2)}) collective-permute-start(f32[3,3,1,2,128]{4,3,0,2,1:T(2,128)S(1)} %pad_maximum_fusion.15), channel_id=1, source_target_pairs={{0,4},{1,5},{2,6},{3,7},{8,12},{9,13},{10,14},{11,15},{16,20},{17,... | collective-permute-start | bytes 27656 | tf_op jit(solution)/shard_map/ppermute | solution.py:22
  46.2 2.0 copy-start.19
  47.6 1.9 copy-start.20
  48.2 6.5 %collective-permute-start.11 = (f32[3,3,3,1,128]{4,3,0,2,1:T(1,128)}, f32[3,3,3,1,128]{4,3,0,2,1:T(1,128)}, u32[]{:S(2)}, u32[]{:S(2)}) collective-permute-start(f32[3,3,3,1,128]{4,3,0,2,1:T(1,128)} %get-tuple-element.27), channel_id=1, source_target_pairs={{1,0},{2,1},{3,2},{5,4},{6,5},{7,6},{9,8},{10,9},{11,10},{13,12},{... | collective-permute-start | bytes 41480 | tf_op jit(solution)/shard_map/ppermute | solution.py:24
  49.5 5.2 %collective-permute-start.10 = (f32[3,3,3,1,128]{4,3,0,2,1:T(1,128)}, f32[3,3,3,1,128]{4,3,0,2,1:T(1,128)}, u32[]{:S(2)}, u32[]{:S(2)}) collective-permute-start(f32[3,3,3,1,128]{4,3,0,2,1:T(1,128)} %get-tuple-element.28), channel_id=1, source_target_pairs={{0,1},{1,2},{2,3},{4,5},{5,6},{6,7},{8,9},{9,10},{10,11},{12,13},{... | collective-permute-start | bytes 41480 | tf_op jit(solution)/shard_map/ppermute | solution.py:22
  56.2 13.2 %copy-start.24 = (f32[3,2]{1,0:T(4,128)S(1)}, f32[3,2]{1,0:T(4,128)}, u32[]{:S(2)}) copy-start(f32[3,2]{1,0:T(4,128)} %copy.31) | copy-start | bytes 76
  62.6 6.8 %copy-start.13 = (f32[6,2,128]{2,1,0:T(2,128)S(1)}, f32[6,2,128]{2,1,0:T(2,128)}, u32[]{:S(2)}) copy-start(f32[6,2,128]{2,1,0:T(2,128)} %copy-done.12) | copy-start | bytes 18436
  70.1 23.1 %copy-start.17 = (f32[1,2,128]{2,1,0:T(2,128)}, f32[1,2,128]{2,1,0:T(2,128)S(1)}, u32[]{:S(2)}) copy-start(f32[1,2,128]{2,1,0:T(2,128)S(1)} %get-tuple-element.15) | copy-start | bytes 3076
  70.1 5.9 %collective-permute-start.13 = (f32[1,1,1,2,128]{4,3,2,1,0:T(2,128)S(1)}, f32[1,1,1,2,128]{4,3,2,1,0:T(2,128)S(1)}, u32[]{:S(2)}, u32[]{:S(2)}) collective-permute-start(f32[1,1,1,2,128]{4,3,2,1,0:T(2,128)S(1)} %bitcast.159), channel_id=1, source_target_pairs={{8,0},{16,8},{24,16},{9,1},{17,9},{25,17},{10,2},{18,10},{26,18},{... | collective-permute-start | bytes 3080 | tf_op jit(solution)/shard_map/ppermute | solution.py:24
  71.4 5.9 %collective-permute-start.12 = (f32[1,1,1,2,128]{4,3,2,1,0:T(2,128)S(1)}, f32[1,1,1,2,128]{4,3,2,1,0:T(2,128)S(1)}, u32[]{:S(2)}, u32[]{:S(2)}) collective-permute-start(f32[1,1,1,2,128]{4,3,2,1,0:T(2,128)S(1)} %bitcast.160), channel_id=1, source_target_pairs={{0,8},{8,16},{16,24},{1,9},{9,17},{17,25},{2,10},{10,18},{18,26},{... | collective-permute-start | bytes 3080 | tf_op jit(solution)/shard_map/ppermute | solution.py:22
  77.3 5.8 %collective-permute-start.15 = (f32[1,3,1,2,128]{4,3,2,1,0:T(2,128)S(1)}, f32[1,3,1,2,128]{4,3,2,1,0:T(2,128)S(1)}, u32[]{:S(2)}, u32[]{:S(2)}) collective-permute-start(f32[1,3,1,2,128]{4,3,2,1,0:T(2,128)S(1)} %pad_maximum_fusion.20), channel_id=1, source_target_pairs={{4,0},{5,1},{6,2},{7,3},{12,8},{13,9},{14,10},{15,11},{20,16},{21,... | collective-permute-start | bytes 9224 | tf_op jit(solution)/shard_map/ppermute | solution.py:24
  78.6 5.9 %collective-permute-start.14 = (f32[1,3,1,2,128]{4,3,2,1,0:T(2,128)S(1)}, f32[1,3,1,2,128]{4,3,2,1,0:T(2,128)S(1)}, u32[]{:S(2)}, u32[]{:S(2)}) collective-permute-start(f32[1,3,1,2,128]{4,3,2,1,0:T(2,128)S(1)} %pad_maximum_fusion.20), channel_id=1, source_target_pairs={{0,4},{1,5},{2,6},{3,7},{8,12},{9,13},{10,14},{11,15},{16,20},{17,... | collective-permute-start | bytes 9224 | tf_op jit(solution)/shard_map/ppermute | solution.py:22
  84.5 2.8 collective-permute-start.16
  86.0 6.6 %collective-permute-start.17 = (f32[1,3,3,1,128]{4,3,2,1,0:T(1,128)S(1)}, f32[1,3,3,1,128]{4,3,2,1,0:T(1,128)S(1)}, u32[]{:S(2)}, u32[]{:S(2)}) collective-permute-start(f32[1,3,3,1,128]{4,3,2,1,0:T(1,128)S(1)} %get-tuple-element.40), channel_id=1, source_target_pairs={{1,0},{2,1},{3,2},{5,4},{6,5},{7,6},{9,8},{10,9},{11,10},{13,12},{... | collective-permute-start | bytes 13832 | tf_op jit(solution)/shard_map/ppermute | solution.py:24
  95.3 2.2 copy-start.6
  95.3 2.2 copy-start.18
  95.3 2.2 copy-start.23
  147.5 21.2 %copy-start.8 = (f32[1,2,128]{2,1,0:T(2,128)}, f32[1,2,128]{2,1,0:T(2,128)S(1)}, u32[]{:S(2)}) copy-start(f32[1,2,128]{2,1,0:T(2,128)S(1)} %bitcast_divide_fusion.1) | copy-start | bytes 3076
  147.5 5.8 %collective-permute-start.19 = (f32[1,1,1,2,128]{4,3,2,1,0:T(2,128)S(1)}, f32[1,1,1,2,128]{4,3,2,1,0:T(2,128)S(1)}, u32[]{:S(2)}, u32[]{:S(2)}) collective-permute-start(f32[1,1,1,2,128]{4,3,2,1,0:T(2,128)S(1)} %bitcast.148), channel_id=1, source_target_pairs={{8,0},{16,8},{24,16},{9,1},{17,9},{25,17},{10,2},{18,10},{26,18},{... | collective-permute-start | bytes 3080 | tf_op jit(solution)/shard_map/ppermute | solution.py:24
  148.7 5.8 %collective-permute-start.18 = (f32[1,1,1,2,128]{4,3,2,1,0:T(2,128)S(1)}, f32[1,1,1,2,128]{4,3,2,1,0:T(2,128)S(1)}, u32[]{:S(2)}, u32[]{:S(2)}) collective-permute-start(f32[1,1,1,2,128]{4,3,2,1,0:T(2,128)S(1)} %bitcast.149), channel_id=1, source_target_pairs={{0,8},{8,16},{16,24},{1,9},{9,17},{17,25},{2,10},{10,18},{18,26},{... | collective-permute-start | bytes 3080 | tf_op jit(solution)/shard_map/ppermute | solution.py:22
  154.6 5.8 %collective-permute-start.21 = (f32[1,3,1,2,128]{4,3,2,1,0:T(2,128)S(1)}, f32[1,3,1,2,128]{4,3,2,1,0:T(2,128)S(1)}, u32[]{:S(2)}, u32[]{:S(2)}) collective-permute-start(f32[1,3,1,2,128]{4,3,2,1,0:T(2,128)S(1)} %pad_maximum_fusion.21), channel_id=1, source_target_pairs={{4,0},{5,1},{6,2},{7,3},{12,8},{13,9},{14,10},{15,11},{20,16},{21,... | collective-permute-start | bytes 9224 | tf_op jit(solution)/shard_map/ppermute | solution.py:24
  155.9 5.9 %collective-permute-start.20 = (f32[1,3,1,2,128]{4,3,2,1,0:T(2,128)S(1)}, f32[1,3,1,2,128]{4,3,2,1,0:T(2,128)S(1)}, u32[]{:S(2)}, u32[]{:S(2)}) collective-permute-start(f32[1,3,1,2,128]{4,3,2,1,0:T(2,128)S(1)} %pad_maximum_fusion.21), channel_id=1, source_target_pairs={{0,4},{1,5},{2,6},{3,7},{8,12},{9,13},{10,14},{11,15},{16,20},{17,... | collective-permute-start | bytes 9224 | tf_op jit(solution)/shard_map/ppermute | solution.py:22
  161.7 2.6 collective-permute-start.22
  163.0 5.6 %collective-permute-start.23 = (f32[1,3,3,1,128]{4,3,2,1,0:T(1,128)S(1)}, f32[1,3,3,1,128]{4,3,2,1,0:T(1,128)S(1)}, u32[]{:S(2)}, u32[]{:S(2)}) collective-permute-start(f32[1,3,3,1,128]{4,3,2,1,0:T(1,128)S(1)} %get-tuple-element.36), channel_id=1, source_target_pairs={{1,0},{2,1},{3,2},{5,4},{6,5},{7,6},{9,8},{10,9},{11,10},{13,12},{... | collective-permute-start | bytes 13832 | tf_op jit(solution)/shard_map/ppermute | solution.py:24
  171.9 2.2 copy-start.9
  171.9 2.2 copy-start.26
  227.8 14.3 %copy-start.15 = (f32[1,2,128]{2,1,0:T(2,128)}, f32[1,2,128]{2,1,0:T(2,128)S(1)}, u32[]{:S(2)}) copy-start(f32[1,2,128]{2,1,0:T(2,128)S(1)} %get-tuple-element.12) | copy-start | bytes 3076
  227.9 5.8 %collective-permute-start.25 = (f32[1,1,1,2,128]{4,3,2,1,0:T(2,128)S(1)}, f32[1,1,1,2,128]{4,3,2,1,0:T(2,128)S(1)}, u32[]{:S(2)}, u32[]{:S(2)}) collective-permute-start(f32[1,1,1,2,128]{4,3,2,1,0:T(2,128)S(1)} %bitcast.154), channel_id=1, source_target_pairs={{8,0},{16,8},{24,16},{9,1},{17,9},{25,17},{10,2},{18,10},{26,18},{... | collective-permute-start | bytes 3080 | tf_op jit(solution)/shard_map/ppermute | solution.py:24
  229.1 5.8 %collective-permute-start.24 = (f32[1,1,1,2,128]{4,3,2,1,0:T(2,128)S(1)}, f32[1,1,1,2,128]{4,3,2,1,0:T(2,128)S(1)}, u32[]{:S(2)}, u32[]{:S(2)}) collective-permute-start(f32[1,1,1,2,128]{4,3,2,1,0:T(2,128)S(1)} %bitcast.155), channel_id=1, source_target_pairs={{0,8},{8,16},{16,24},{1,9},{9,17},{17,25},{2,10},{10,18},{18,26},{... | collective-permute-start | bytes 3080 | tf_op jit(solution)/shard_map/ppermute | solution.py:22
  233.7 10.9 %copy-start.31 = (f32[1,1,1,2,128]{4,3,2,1,0:T(2,128)}, f32[1,1,1,2,128]{4,3,2,1,0:T(2,128)S(1)}, u32[]{:S(2)}) copy-start(f32[1,1,1,2,128]{4,3,2,1,0:T(2,128)S(1)} %collective-permute-done.25) | copy-start | bytes 3076
  235.0 9.7 %copy-start.32 = (f32[1,1,1,2,128]{4,3,2,1,0:T(2,128)}, f32[1,1,1,2,128]{4,3,2,1,0:T(2,128)S(1)}, u32[]{:S(2)}) copy-start(f32[1,1,1,2,128]{4,3,2,1,0:T(2,128)S(1)} %collective-permute-done.24) | copy-start | bytes 3076
  235.0 5.8 %collective-permute-start.27 = (f32[1,3,1,2,128]{4,3,2,1,0:T(2,128)S(1)}, f32[1,3,1,2,128]{4,3,2,1,0:T(2,128)S(1)}, u32[]{:S(2)}, u32[]{:S(2)}) collective-permute-start(f32[1,3,1,2,128]{4,3,2,1,0:T(2,128)S(1)} %pad_maximum_fusion.22), channel_id=1, source_target_pairs={{4,0},{5,1},{6,2},{7,3},{12,8},{13,9},{14,10},{15,11},{20,16},{21,... | collective-permute-start | bytes 9224 | tf_op jit(solution)/shard_map/ppermute | solution.py:24
  236.3 5.9 %collective-permute-start.26 = (f32[1,3,1,2,128]{4,3,2,1,0:T(2,128)S(1)}, f32[1,3,1,2,128]{4,3,2,1,0:T(2,128)S(1)}, u32[]{:S(2)}, u32[]{:S(2)}) collective-permute-start(f32[1,3,1,2,128]{4,3,2,1,0:T(2,128)S(1)} %pad_maximum_fusion.22), channel_id=1, source_target_pairs={{0,4},{1,5},{2,6},{3,7},{8,12},{9,13},{10,14},{11,15},{16,20},{17,... | collective-permute-start | bytes 9224 | tf_op jit(solution)/shard_map/ppermute | solution.py:22
  240.8 1.9 copy-start.27
  242.7 8.7 %collective-permute-start.28 = (f32[1,3,3,1,128]{4,3,2,1,0:T(1,128)}, f32[1,3,3,1,128]{4,3,2,1,0:T(1,128)}, u32[]{:S(2)}, u32[]{:S(2)}) collective-permute-start(f32[1,3,3,1,128]{4,3,2,1,0:T(1,128)} %get-tuple-element.31), channel_id=1, source_target_pairs={{0,1},{1,2},{2,3},{4,5},{5,6},{6,7},{8,9},{9,10},{10,11},{12,13},{... | collective-permute-start | bytes 13832 | tf_op jit(solution)/shard_map/ppermute | solution.py:22
  244.6 6.8 %collective-permute-start.29 = (f32[1,3,3,1,128]{4,3,2,1,0:T(1,128)}, f32[1,3,3,1,128]{4,3,2,1,0:T(1,128)}, u32[]{:S(2)}, u32[]{:S(2)}) collective-permute-start(f32[1,3,3,1,128]{4,3,2,1,0:T(1,128)} %get-tuple-element.32), channel_id=1, source_target_pairs={{1,0},{2,1},{3,2},{5,4},{6,5},{7,6},{9,8},{10,9},{11,10},{13,12},{... | collective-permute-start | bytes 13832 | tf_op jit(solution)/shard_map/ppermute | solution.py:24
  256.9 2.3 copy-start.16
  256.9 2.3 copy-start.34
  259.1 59.5 %copy-start.4 = (f32[3,2,128]{2,1,0:T(2,128)S(1)}, f32[3,2,128]{2,1,0:T(2,128)}, u32[]{:S(2)}) copy-start(f32[3,2,128]{2,1,0:T(2,128)} %copy-done.3) | copy-start | bytes 9220
  259.1 59.5 %copy-start.7 = (f32[2,128]{1,0:T(2,128)S(1)}, f32[2,128]{1,0:T(2,128)}, u32[]{:S(2)}) copy-start(f32[2,128]{1,0:T(2,128)} %copy-done.5) | copy-start | bytes 3076
  259.1 59.5 %copy-start.11 = (f32[3,1,1,2,128]{4,3,2,1,0:T(2,128)S(1)}, f32[3,1,1,2,128]{4,3,2,1,0:T(2,128)}, u32[]{:S(2)}) copy-start(f32[3,1,1,2,128]{4,3,2,1,0:T(2,128)} %param.4) | copy-start | bytes 9220
  259.2 59.5 %copy-start.14 = (f32[6,2,128]{2,1,0:T(2,128)S(1)}, f32[6,2,128]{2,1,0:T(2,128)}, u32[]{:S(2)}) copy-start(f32[6,2,128]{2,1,0:T(2,128)} %copy-done.12) | copy-start | bytes 18436
  259.2 59.5 %copy-start.25 = (f32[3,2]{1,0:T(4,128)S(1)}, f32[3,2]{1,0:T(4,128)}, u32[]{:S(2)}) copy-start(f32[3,2]{1,0:T(4,128)} %copy.31) | copy-start | bytes 76
  313.4 5.9 %copy-start.35 = (f32[1,2,128]{2,1,0:T(2,128)}, f32[1,2,128]{2,1,0:T(2,128)S(1)}, u32[]{:S(2)}) copy-start(f32[1,2,128]{2,1,0:T(2,128)S(1)} %multiply_add_fusion.1) | copy-start | bytes 3076
  (3 other events, 2.6 us)
where the time goes:
time: 322 us; the launch traced here: 319 us
  blocking collectives  132 us (41%)
  starting transfers between devices  76 us (24%)
  other arithmetic  41.9 us (13%)
  local copies, waits for them, and re-layouts  32.6 us (10%)
  waiting for transfers between devices  25.9 us (8%)
  between operations  11.2 us (3%)
    psum x3, blocking collectives, paired_sums(): total = lax.psum(pair, ('gx', 'gy', 'gz'))  132 us
    ppermute x15, starting transfers between devices, with_halo(): lax.ppermute(tail, axis, [(i, (i + 1) % count) for i in range(ends)])  56.6 us
    ppermute x15, starting transfers between devices, with_halo(): lax.ppermute(head, axis, [((i + 1) % count, i) for i in range(ends)])  19.5 us
    another operation x15, local copies, waits for them, and re-layouts, neighbours(): return jnp.stack(blocks, axis=1)  19.3 us
    ppermute x15, waiting for transfers between devices, with_halo(): lax.ppermute(head, axis, [((i + 1) % count, i) for i in range(ends)])  13.5 us
    reduce_sum x6, other arithmetic, wsum(): return jnp.sum(weight[None] * near[:, :, None, :], axis=-1)  12.6 us
    ppermute x15, waiting for transfers between devices, with_halo(): lax.ppermute(tail, axis, [(i, (i + 1) % count) for i in range(ends)])  12.3 us
  transfers between devices with their start and end apart: 30, of which 13 were waited for; matrix products, arithmetic and copies ran while one was open for 2% of the time, Pallas kernels for 0%

commit v1 on v0

--- a/solution.py
+++ b/solution.py
@@ -1,3 +1,4 @@
+import functools
 import jax
 import jax.numpy as jnp
 from jax import lax
@@ -9,6 +10,14 @@
 GRAVITY = 0.1
 GRADIENT_GAIN = 32.0
 AXES = (("gx", 1), ("gy", 2), ("gz", 3))
+
+
+def open_edges_on(xs, axis_name):
+    local_out = lax.all_gather(xs, axis_name)
+    return jnp.sum(local_out, 0)
+
+
+pass_strings_for = functools.partial(open_edges_on, axis_name=("gx", "gy", "gz"))
 
 
 def with_halo(cells, sides, width):
@@ -107,7 +116,7 @@
 
     def paired_sums(residual, precond, applied):
         pair = jnp.stack([jnp.sum(residual * precond), jnp.sum(precond * applied)])
-        total = lax.psum(pair, ("gx", "gy", "gz"))
+        total = pass_strings_for(pair)
         return (total[0], total[1])
 
     pressure = jnp.zeros_like(source)

time: 322 us -> 333 us (1.034)
  other arithmetic: 41.9 us -> 46.9 us
  local copies, waits for them, and re-layouts: 32.6 us -> 37.4 us
    psum x3 -> x0, blocking collectives: 132 us -> none  [paired_sums(): total = lax.psum(pair, ('gx', 'gy', 'gz'))]
    unnamed x0 -> x3, blocking collectives: none -> 132 us
    unnamed x1 -> x4, other arithmetic: 0.66 us -> 7.33 us
    another operation x3 -> x0, other arithmetic: 4.92 us -> none  [paired_sums(): pair = jnp.stack([jnp.sum(residual * precond), jnp.sum(precond * applied)])]
where the time goes in v1:
time: 333 us; the launch traced here: 329 us
  blocking collectives  132 us (40%)
  starting transfers between devices  76.6 us (23%)
  other arithmetic  46.9 us (14%)
  local copies, waits for them, and re-layouts  37.4 us (11%)
  waiting for transfers between devices  25.6 us (8%)
  between operations  11.2 us (3%)
    unnamed x3, blocking collectives  132 us
    ppermute x15, starting transfers between devices, with_halo(): lax.ppermute(tail, axis, [(i, (i + 1) % count) for i in range(ends)])  57.2 us
    another operation x15, local copies, waits for them, and re-layouts, neighbours(): return jnp.stack(blocks, axis=1)  19.9 us
    ppermute x15, starting transfers between devices, with_halo(): lax.ppermute(head, axis, [((i + 1) % count, i) for i in range(ends)])  19.4 us
    ppermute x15, waiting for transfers between devices, with_halo(): lax.ppermute(head, axis, [((i + 1) % count, i) for i in range(ends)])  13.3 us
    reduce_sum x6, other arithmetic, wsum(): return jnp.sum(weight[None] * near[:, :, None, :], axis=-1)  12.5 us
    ppermute x15, waiting for transfers between devices, with_halo(): lax.ppermute(tail, axis, [(i, (i + 1) % count) for i in range(ends)])  12.3 us
    unnamed x4, other arithmetic  7.33 us
  transfers between devices with their start and end apart: 30, of which 13 were waited for; matrix products, arithmetic and copies ran while one was open for 2% of the time, Pallas kernels for 0%

profile of v1, /device:TPU:0, one launch (start us, length us, event | category | flops | bytes accessed | tf_op | source)
XLA Modules:
  0.0 329.4 jit_solution(9682376368374518692)
XLA Ops:
  4.0 5.6 %collective-permute-start = (f32[7,1,1,2,128]{4,0,3,2,1:T(8,128)S(1)}, f32[7,1,1,2,128]{4,0,3,2,1:T(8,128)S(1)}, u32[]{:S(2)}, u32[]{:S(2)}) collective-permute-start(f32[7,1,1,2,128]{4,0,3,2,1:T(8,128)S(1)} %pad_maximum_fusion.19), channel_id=1, source_target_pairs={{0,8},{8,16},{16,24},{1,9},{9,17},{17,25},{2,10},{10,18},{18,26},{... | collective-permute-start | bytes 21512 | tf_op jit(solution)/shard_map/ppermute | solution.py:31
  12.3 4.5 %collective-permute-start.2 = (f32[7,3,1,2,128]{4,0,3,2,1:T(8,128)S(1)}, f32[7,3,1,2,128]{4,0,3,2,1:T(8,128)S(1)}, u32[]{:S(2)}, u32[]{:S(2)}) collective-permute-start(f32[7,3,1,2,128]{4,0,3,2,1:T(8,128)S(1)} %pad_maximum_fusion.11), channel_id=1, source_target_pairs={{0,4},{1,5},{2,6},{3,7},{8,12},{9,13},{10,14},{11,15},{16,20},{17,... | collective-permute-start | bytes 64520 | tf_op jit(solution)/shard_map/ppermute | solution.py:31
  16.9 1.4 collective-permute-done.2
  18.3 1.3 collective-permute-start.4
  19.6 1.3 collective-permute-start.5
  21.0 3.9 %collective-permute-done.5 = f32[7,3,3,1,128]{4,0,3,2,1:T(8,128)S(1)} collective-permute-done((f32[7,3,3,1,128]{4,0,3,2,1:T(8,128)S(1)}, f32[7,3,3,1,128]{4,0,3,2,1:T(8,128)S(1)}, u32[]{:S(2)}, u32[]{:S(2)}) %collective-permute-start.5) | collective-permute-done | bytes 32288 | tf_op jit(solution)/shard_map/ppermute | solution.py:33
  25.3 1.5 broadcast_subtract_fusion
  26.9 1.6 fusion.6
  28.9 1.7 copy-done
  30.7 1.8 multiply_reduce_fusion
  33.9 4.8 %collective-permute-start.6 = (f32[3,1,1,2,128]{4,3,0,2,1:T(2,128)S(1)}, f32[3,1,1,2,128]{4,3,0,2,1:T(2,128)S(1)}, u32[]{:S(2)}, u32[]{:S(2)}) collective-permute-start(f32[3,1,1,2,128]{4,3,0,2,1:T(2,128)S(1)} %bitcast.144), channel_id=1, source_target_pairs={{0,8},{8,16},{16,24},{1,9},{9,17},{17,25},{2,10},{10,18},{18,26},{... | collective-permute-start | bytes 9224 | tf_op jit(solution)/shard_map/ppermute | solution.py:31
  40.0 1.3 collective-permute-start.9
  41.3 4.5 %collective-permute-start.8 = (f32[3,3,1,2,128]{4,3,0,2,1:T(2,128)S(1)}, f32[3,3,1,2,128]{4,3,0,2,1:T(2,128)S(1)}, u32[]{:S(2)}, u32[]{:S(2)}) collective-permute-start(f32[3,3,1,2,128]{4,3,0,2,1:T(2,128)S(1)} %pad_maximum_fusion.15), channel_id=1, source_target_pairs={{0,4},{1,5},{2,6},{3,7},{8,12},{9,13},{10,14},{11,15},{16,20},{17,... | collective-permute-start | bytes 27656 | tf_op jit(solution)/shard_map/ppermute | solution.py:31
  45.9 1.3 collective-permute-done.8
  49.2 3.8 %collective-permute-start.10 = (f32[3,3,3,1,128]{4,3,0,2,1:T(1,128)}, f32[3,3,3,1,128]{4,3,0,2,1:T(1,128)}, u32[]{:S(2)}, u32[]{:S(2)}) collective-permute-start(f32[3,3,3,1,128]{4,3,0,2,1:T(1,128)} %get-tuple-element.28), channel_id=1, source_target_pairs={{0,1},{1,2},{2,3},{4,5},{5,6},{6,7},{8,9},{9,10},{10,11},{12,13},{... | collective-permute-start | bytes 41480 | tf_op jit(solution)/shard_map/ppermute | solution.py:31
  53.0 1.3 copy.31
  54.3 1.5 pad_maximum_fusion.5
  56.5 1.5 stack_reshape.32
  57.9 1.4 constant_dynamic-update-slice_fusion.1
  59.4 1.4 copy.33
  60.8 1.5 stack_reshape.33
  62.3 1.4 constant_dynamic-update-slice_fusion
  65.8 3.3 multiply_reduce_fusion.2
  71.0 4.6 %collective-permute-start.12 = (f32[1,1,1,2,128]{4,3,2,1,0:T(2,128)S(1)}, f32[1,1,1,2,128]{4,3,2,1,0:T(2,128)S(1)}, u32[]{:S(2)}, u32[]{:S(2)}) collective-permute-start(f32[1,1,1,2,128]{4,3,2,1,0:T(2,128)S(1)} %bitcast.160), channel_id=1, source_target_pairs={{0,8},{8,16},{16,24},{1,9},{9,17},{17,25},{2,10},{10,18},{18,26},{... | collective-permute-start | bytes 3080 | tf_op jit(solution)/shard_map/ppermute | solution.py:31
  78.3 4.5 %collective-permute-start.14 = (f32[1,3,1,2,128]{4,3,2,1,0:T(2,128)S(1)}, f32[1,3,1,2,128]{4,3,2,1,0:T(2,128)S(1)}, u32[]{:S(2)}, u32[]{:S(2)}) collective-permute-start(f32[1,3,1,2,128]{4,3,2,1,0:T(2,128)S(1)} %pad_maximum_fusion.20), channel_id=1, source_target_pairs={{0,4},{1,5},{2,6},{3,7},{8,12},{9,13},{10,14},{11,15},{16,20},{17,... | collective-permute-start | bytes 9224 | tf_op jit(solution)/shard_map/ppermute | solution.py:31
  84.7 2.1 collective-permute-start.16
  88.1 5.1 %collective-permute-done.17 = f32[1,3,3,1,128]{4,3,2,1,0:T(1,128)} collective-permute-done((f32[1,3,3,1,128]{4,3,2,1,0:T(1,128)}, f32[1,3,3,1,128]{4,3,2,1,0:T(1,128)}, u32[]{:S(2)}, u32[]{:S(2)}) %collective-permute-start.17) | collective-permute-done | bytes 4640 | tf_op jit(solution)/shard_map/ppermute | solution.py:33
  93.2 1.4 maximum_maximum_fusion.2
  95.3 1.3 stack_reshape.34
  97.4 1.4 multiply_reduce_fusion.5
  100.7 2.6 maximum_dynamic-update-slice_fusion
  103.3 43.4 %all-reduce = f32[64]{0:T(128)} all-reduce(f32[64]{0:T(128)} %maximum_dynamic-update-slice_fusion), channel_id=2, replica_groups=mesh['gx'=4,'gy'=2,'gz'=4] {'gx','gy','gz'}, use_global_device_ids=true, to_apply=%add | all-reduce | flops 64 | bytes 512
  146.6 1.3 reshape.393
  149.2 1.4 fusion.36
  153.9 4.5 %collective-permute-start.18 = (f32[1,1,1,2,128]{4,3,2,1,0:T(2,128)S(1)}, f32[1,1,1,2,128]{4,3,2,1,0:T(2,128)S(1)}, u32[]{:S(2)}, u32[]{:S(2)}) collective-permute-start(f32[1,1,1,2,128]{4,3,2,1,0:T(2,128)S(1)} %bitcast.149), channel_id=1, source_target_pairs={{0,8},{8,16},{16,24},{1,9},{9,17},{17,25},{2,10},{10,18},{18,26},{... | collective-permute-start | bytes 3080 | tf_op jit(solution)/shard_map/ppermute | solution.py:31
  161.0 4.5 %collective-permute-start.20 = (f32[1,3,1,2,128]{4,3,2,1,0:T(2,128)S(1)}, f32[1,3,1,2,128]{4,3,2,1,0:T(2,128)S(1)}, u32[]{:S(2)}, u32[]{:S(2)}) collective-permute-start(f32[1,3,1,2,128]{4,3,2,1,0:T(2,128)S(1)} %pad_maximum_fusion.21), channel_id=1, source_target_pairs={{0,4},{1,5},{2,6},{3,7},{8,12},{9,13},{10,14},{11,15},{16,20},{17,... | collective-permute-start | bytes 9224 | tf_op jit(solution)/shard_map/ppermute | solution.py:31
  168.1 1.3 collective-permute-start.23
  169.5 4.3 %collective-permute-done.23 = f32[1,3,3,1,128]{4,3,2,1,0:T(1,128)S(1)} collective-permute-done((f32[1,3,3,1,128]{4,3,2,1,0:T(1,128)S(1)}, f32[1,3,3,1,128]{4,3,2,1,0:T(1,128)S(1)}, u32[]{:S(2)}, u32[]{:S(2)}) %collective-permute-start.23) | collective-permute-done | bytes 4640 | tf_op jit(solution)/shard_map/ppermute | solution.py:33
  174.3 1.4 stack_reshape.37
  175.7 1.3 stack_reshape.36
  177.8 1.4 multiply_reduce_fusion.4
  179.3 1.4 multiply_reduce_fusion.10
  181.2 2.6 maximum_dynamic-update-slice_fusion.1
  183.8 43.4 %all-reduce.1 = f32[64]{0:T(128)} all-reduce(f32[64]{0:T(128)} %maximum_dynamic-update-slice_fusion.1), channel_id=3, replica_groups=mesh['gx'=4,'gy'=2,'gz'=4] {'gx','gy','gz'}, use_global_device_ids=true, to_apply=%add.1 | all-reduce | flops 64 | bytes 512
  227.2 1.4 reshape.394
  229.8 1.4 fusion.35
  238.2 4.5 %collective-permute-start.24 = (f32[1,1,1,2,128]{4,3,2,1,0:T(2,128)S(1)}, f32[1,1,1,2,128]{4,3,2,1,0:T(2,128)S(1)}, u32[]{:S(2)}, u32[]{:S(2)}) collective-permute-start(f32[1,1,1,2,128]{4,3,2,1,0:T(2,128)S(1)} %bitcast.155), channel_id=1, source_target_pairs={{0,8},{8,16},{16,24},{1,9},{9,17},{17,25},{2,10},{10,18},{18,26},{... | collective-permute-start | bytes 3080 | tf_op jit(solution)/shard_map/ppermute | solution.py:31
  245.3 4.5 %collective-permute-start.26 = (f32[1,3,1,2,128]{4,3,2,1,0:T(2,128)S(1)}, f32[1,3,1,2,128]{4,3,2,1,0:T(2,128)S(1)}, u32[]{:S(2)}, u32[]{:S(2)}) collective-permute-start(f32[1,3,1,2,128]{4,3,2,1,0:T(2,128)S(1)} %pad_maximum_fusion.22), channel_id=1, source_target_pairs={{0,4},{1,5},{2,6},{3,7},{8,12},{9,13},{10,14},{11,15},{16,20},{17,... | collective-permute-start | bytes 9224 | tf_op jit(solution)/shard_map/ppermute | solution.py:31
  251.8 1.9 collective-permute-start.28
  253.7 1.5 collective-permute-start.29
  255.1 1.3 stack.113
  256.5 1.3 stack.112
  257.8 1.3 stack.116
  259.2 1.3 stack.115
  260.5 1.4 maximum_maximum_fusion.4
  261.9 1.3 stack.119
  263.3 1.3 stack_reshape.39
  264.6 1.3 stack.118
  265.9 1.3 stack_reshape.38
  268.1 1.4 multiply_reduce_fusion.3
  269.6 1.3 multiply_reduce_fusion.8
  270.9 1.5 maximum_dynamic-update-slice_fusion.2
  272.4 44.9 %all-reduce.2 = f32[64]{0:T(128)S(1)} all-reduce(f32[64]{0:T(128)S(1)} %maximum_dynamic-update-slice_fusion.2), channel_id=4, replica_groups=mesh['gx'=4,'gy'=2,'gz'=4] {'gx','gy','gz'}, use_global_device_ids=true, to_apply=%add.2 | all-reduce | flops 64 | bytes 512
  325.6 3.1 multiply_reduce_fusion.1
  (179 shorter events, 49.5 us)
Async XLA Ops:
  2.7 7.6 %collective-permute-start.1 = (f32[7,1,1,2,128]{4,0,3,2,1:T(8,128)S(1)}, f32[7,1,1,2,128]{4,0,3,2,1:T(8,128)S(1)}, u32[]{:S(2)}, u32[]{:S(2)}) collective-permute-start(f32[7,1,1,2,128]{4,0,3,2,1:T(8,128)S(1)} %pad_maximum_fusion.19), channel_id=1, source_target_pairs={{8,0},{16,8},{24,16},{9,1},{17,9},{25,17},{10,2},{18,10},{26,18},{... | collective-permute-start | bytes 21512 | tf_op jit(solution)/shard_map/ppermute | solution.py:33
  4.0 6.9 %collective-permute-start = (f32[7,1,1,2,128]{4,0,3,2,1:T(8,128)S(1)}, f32[7,1,1,2,128]{4,0,3,2,1:T(8,128)S(1)}, u32[]{:S(2)}, u32[]{:S(2)}) collective-permute-start(f32[7,1,1,2,128]{4,0,3,2,1:T(8,128)S(1)} %pad_maximum_fusion.19), channel_id=1, source_target_pairs={{0,8},{8,16},{16,24},{1,9},{9,17},{17,25},{2,10},{10,18},{18,26},{... | collective-permute-start | bytes 21512 | tf_op jit(solution)/shard_map/ppermute | solution.py:31
  10.3 22.1 %copy-start.21 = (f32[2,128]{1,0:T(2,128)}, f32[2,128]{1,0:T(2,128)S(1)}, u32[]{:S(2)}) copy-start(f32[2,128]{1,0:T(2,128)S(1)} %compare_convert_fusion.1) | copy-start | bytes 3076
  11.0 5.9 %collective-permute-start.3 = (f32[7,3,1,2,128]{4,0,3,2,1:T(8,128)S(1)}, f32[7,3,1,2,128]{4,0,3,2,1:T(8,128)S(1)}, u32[]{:S(2)}, u32[]{:S(2)}) collective-permute-start(f32[7,3,1,2,128]{4,0,3,2,1:T(8,128)S(1)} %pad_maximum_fusion.11), channel_id=1, source_target_pairs={{4,0},{5,1},{6,2},{7,3},{12,8},{13,9},{14,10},{15,11},{20,16},{21,... | collective-permute-start | bytes 64520 | tf_op jit(solution)/shard_map/ppermute | solution.py:33
  12.3 6.1 %collective-permute-start.2 = (f32[7,3,1,2,128]{4,0,3,2,1:T(8,128)S(1)}, f32[7,3,1,2,128]{4,0,3,2,1:T(8,128)S(1)}, u32[]{:S(2)}, u32[]{:S(2)}) collective-permute-start(f32[7,3,1,2,128]{4,0,3,2,1:T(8,128)S(1)} %pad_maximum_fusion.11), channel_id=1, source_target_pairs={{0,4},{1,5},{2,6},{3,7},{8,12},{9,13},{10,14},{11,15},{16,20},{17,... | collective-permute-start | bytes 64520 | tf_op jit(solution)/shard_map/ppermute | solution.py:31
  18.3 2.6 collective-permute-start.4
  19.6 5.3 %collective-permute-start.5 = (f32[7,3,3,1,128]{4,0,3,2,1:T(8,128)S(1)}, f32[7,3,3,1,128]{4,0,3,2,1:T(8,128)S(1)}, u32[]{:S(2)}, u32[]{:S(2)}) collective-permute-start(f32[7,3,3,1,128]{4,0,3,2,1:T(8,128)S(1)} %get-tuple-element.24), channel_id=1, source_target_pairs={{1,0},{2,1},{3,2},{5,4},{6,5},{7,6},{9,8},{10,9},{11,10},{13,12},{... | collective-permute-start | bytes 96776 | tf_op jit(solution)/shard_map/ppermute | solution.py:33
  21.0 5.9 %copy-start.30 = (f32[3,2]{0,1:T(2,128)}, f32[3,2]{0,1:T(2,128)S(1)}, u32[]{:S(2)}) copy-start(f32[3,2]{0,1:T(2,128)S(1)} %add_convert_fusion) | copy-start | bytes 76
  25.3 3.2 copy-start.2
  28.5 40.7 %copy-start.5 = (f32[2,128]{1,0:T(2,128)}, f32[2,128]{1,0:T(2,128)S(1)}, u32[]{:S(2)}) copy-start(f32[2,128]{1,0:T(2,128)S(1)} %get-tuple-element.17) | copy-start | bytes 3076
  30.7 1.8 copy-start.38
  32.5 15.4 %copy-start.12 = (f32[6,2,128]{2,1,0:T(2,128)}, f32[6,2,128]{2,1,0:T(2,128)S(1)}, u32[]{:S(2)}) copy-start(f32[6,2,128]{2,1,0:T(2,128)S(1)} %multiply_reduce_fusion) | copy-start | bytes 18436
  32.5 36.6 %copy-start.10 = (f32[3,1,1,2,128]{4,3,2,1,0:T(2,128)S(1)}, f32[3,1,1,2,128]{4,3,2,1,0:T(2,128)}, u32[]{:S(2)}) copy-start(f32[3,1,1,2,128]{4,3,2,1,0:T(2,128)} %param.4) | copy-start | bytes 9220
  32.6 62.0 %copy-start.3 = (f32[3,2,128]{2,1,0:T(2,128)}, f32[3,2,128]{2,1,0:T(2,128)S(1)}, u32[]{:S(2)}) copy-start(f32[3,2,128]{2,1,0:T(2,128)S(1)} %fusion.20) | copy-start | bytes 9220
  32.6 6.1 %collective-permute-start.7 = (f32[3,1,1,2,128]{4,3,0,2,1:T(2,128)S(1)}, f32[3,1,1,2,128]{4,3,0,2,1:T(2,128)S(1)}, u32[]{:S(2)}, u32[]{:S(2)}) collective-permute-start(f32[3,1,1,2,128]{4,3,0,2,1:T(2,128)S(1)} %bitcast.143), channel_id=1, source_target_pairs={{8,0},{16,8},{24,16},{9,1},{17,9},{25,17},{10,2},{18,10},{26,18},{... | collective-permute-start | bytes 9224 | tf_op jit(solution)/shard_map/ppermute | solution.py:33
  33.9 6.1 %collective-permute-start.6 = (f32[3,1,1,2,128]{4,3,0,2,1:T(2,128)S(1)}, f32[3,1,1,2,128]{4,3,0,2,1:T(2,128)S(1)}, u32[]{:S(2)}, u32[]{:S(2)}) collective-permute-start(f32[3,1,1,2,128]{4,3,0,2,1:T(2,128)S(1)} %bitcast.144), channel_id=1, source_target_pairs={{0,8},{8,16},{16,24},{1,9},{9,17},{17,25},{2,10},{10,18},{18,26},{... | collective-permute-start | bytes 9224 | tf_op jit(solution)/shard_map/ppermute | solution.py:31
  40.0 9.2 %copy-start.22 = (f32[3,1,1,2,128]{4,3,0,2,1:T(2,128)}, f32[3,1,1,2,128]{4,3,0,2,1:T(2,128)S(1)}, u32[]{:S(2)}) copy-start(f32[3,1,1,2,128]{4,3,0,2,1:T(2,128)S(1)} %collective-permute-done.6) | copy-start | bytes 9220
  40.0 5.9 %collective-permute-start.9 = (f32[3,3,1,2,128]{4,3,0,2,1:T(2,128)S(1)}, f32[3,3,1,2,128]{4,3,0,2,1:T(2,128)S(1)}, u32[]{:S(2)}, u32[]{:S(2)}) collective-permute-start(f32[3,3,1,2,128]{4,3,0,2,1:T(2,128)S(1)} %pad_maximum_fusion.15), channel_id=1, source_target_pairs={{4,0},{5,1},{6,2},{7,3},{12,8},{13,9},{14,10},{15,11},{20,16},{21,... | collective-permute-start | bytes 27656 | tf_op jit(solution)/shard_map/ppermute | solution.py:33
  41.3 5.9 %collective-permute-start.8 = (f32[3,3,1,2,128]{4,3,0,2,1:T(2,128)S(1)}, f32[3,3,1,2,128]{4,3,0,2,1:T(2,128)S(1)}, u32[]{:S(2)}, u32[]{:S(2)}) collective-permute-start(f32[3,3,1,2,128]{4,3,0,2,1:T(2,128)S(1)} %pad_maximum_fusion.15), channel_id=1, source_target_pairs={{0,4},{1,5},{2,6},{3,7},{8,12},{9,13},{10,14},{11,15},{16,20},{17,... | collective-permute-start | bytes 27656 | tf_op jit(solution)/shard_map/ppermute | solution.py:31
  45.9 2.0 copy-start.19
  47.2 1.9 copy-start.20
  47.9 6.5 %collective-permute-start.11 = (f32[3,3,3,1,128]{4,3,0,2,1:T(1,128)}, f32[3,3,3,1,128]{4,3,0,2,1:T(1,128)}, u32[]{:S(2)}, u32[]{:S(2)}) collective-permute-start(f32[3,3,3,1,128]{4,3,0,2,1:T(1,128)} %get-tuple-element.27), channel_id=1, source_target_pairs={{1,0},{2,1},{3,2},{5,4},{6,5},{7,6},{9,8},{10,9},{11,10},{13,12},{... | collective-permute-start | bytes 41480 | tf_op jit(solution)/shard_map/ppermute | solution.py:33
  49.2 5.2 %collective-permute-start.10 = (f32[3,3,3,1,128]{4,3,0,2,1:T(1,128)}, f32[3,3,3,1,128]{4,3,0,2,1:T(1,128)}, u32[]{:S(2)}, u32[]{:S(2)}) collective-permute-start(f32[3,3,3,1,128]{4,3,0,2,1:T(1,128)} %get-tuple-element.28), channel_id=1, source_target_pairs={{0,1},{1,2},{2,3},{4,5},{5,6},{6,7},{8,9},{9,10},{10,11},{12,13},{... | collective-permute-start | bytes 41480 | tf_op jit(solution)/shard_map/ppermute | solution.py:31
  55.8 13.2 %copy-start.24 = (f32[3,2]{1,0:T(4,128)S(1)}, f32[3,2]{1,0:T(4,128)}, u32[]{:S(2)}) copy-start(f32[3,2]{1,0:T(4,128)} %copy.31) | copy-start | bytes 76
  62.3 6.8 %copy-start.13 = (f32[6,2,128]{2,1,0:T(2,128)S(1)}, f32[6,2,128]{2,1,0:T(2,128)}, u32[]{:S(2)}) copy-start(f32[6,2,128]{2,1,0:T(2,128)} %copy-done.12) | copy-start | bytes 18436
  69.8 24.8 %copy-start.17 = (f32[1,2,128]{2,1,0:T(2,128)}, f32[1,2,128]{2,1,0:T(2,128)S(1)}, u32[]{:S(2)}) copy-start(f32[1,2,128]{2,1,0:T(2,128)S(1)} %get-tuple-element.15) | copy-start | bytes 3076
  69.8 5.9 %collective-permute-start.13 = (f32[1,1,1,2,128]{4,3,2,1,0:T(2,128)S(1)}, f32[1,1,1,2,128]{4,3,2,1,0:T(2,128)S(1)}, u32[]{:S(2)}, u32[]{:S(2)}) collective-permute-start(f32[1,1,1,2,128]{4,3,2,1,0:T(2,128)S(1)} %bitcast.159), channel_id=1, source_target_pairs={{8,0},{16,8},{24,16},{9,1},{17,9},{25,17},{10,2},{18,10},{26,18},{... | collective-permute-start | bytes 3080 | tf_op jit(solution)/shard_map/ppermute | solution.py:33
  71.0 5.9 %collective-permute-start.12 = (f32[1,1,1,2,128]{4,3,2,1,0:T(2,128)S(1)}, f32[1,1,1,2,128]{4,3,2,1,0:T(2,128)S(1)}, u32[]{:S(2)}, u32[]{:S(2)}) collective-permute-start(f32[1,1,1,2,128]{4,3,2,1,0:T(2,128)S(1)} %bitcast.160), channel_id=1, source_target_pairs={{0,8},{8,16},{16,24},{1,9},{9,17},{17,25},{2,10},{10,18},{18,26},{... | collective-permute-start | bytes 3080 | tf_op jit(solution)/shard_map/ppermute | solution.py:31
  75.7 9.0 %copy-start.31 = (f32[1,1,1,2,128]{4,3,2,1,0:T(2,128)}, f32[1,1,1,2,128]{4,3,2,1,0:T(2,128)S(1)}, u32[]{:S(2)}) copy-start(f32[1,1,1,2,128]{4,3,2,1,0:T(2,128)S(1)} %collective-permute-done.13) | copy-start | bytes 3076
  77.0 7.8 %copy-start.33 = (f32[1,1,1,2,128]{4,3,2,1,0:T(2,128)}, f32[1,1,1,2,128]{4,3,2,1,0:T(2,128)S(1)}, u32[]{:S(2)}) copy-start(f32[1,1,1,2,128]{4,3,2,1,0:T(2,128)S(1)} %collective-permute-done.12) | copy-start | bytes 3076
  77.0 5.8 %collective-permute-start.15 = (f32[1,3,1,2,128]{4,3,2,1,0:T(2,128)S(1)}, f32[1,3,1,2,128]{4,3,2,1,0:T(2,128)S(1)}, u32[]{:S(2)}, u32[]{:S(2)}) collective-permute-start(f32[1,3,1,2,128]{4,3,2,1,0:T(2,128)S(1)} %pad_maximum_fusion.20), channel_id=1, source_target_pairs={{4,0},{5,1},{6,2},{7,3},{12,8},{13,9},{14,10},{15,11},{20,16},{21,... | collective-permute-start | bytes 9224 | tf_op jit(solution)/shard_map/ppermute | solution.py:33
  78.3 5.9 %collective-permute-start.14 = (f32[1,3,1,2,128]{4,3,2,1,0:T(2,128)S(1)}, f32[1,3,1,2,128]{4,3,2,1,0:T(2,128)S(1)}, u32[]{:S(2)}, u32[]{:S(2)}) collective-permute-start(f32[1,3,1,2,128]{4,3,2,1,0:T(2,128)S(1)} %pad_maximum_fusion.20), channel_id=1, source_target_pairs={{0,4},{1,5},{2,6},{3,7},{8,12},{9,13},{10,14},{11,15},{16,20},{17,... | collective-permute-start | bytes 9224 | tf_op jit(solution)/shard_map/ppermute | solution.py:31
  84.7 3.4 %collective-permute-start.16 = (f32[1,3,3,1,128]{4,3,2,1,0:T(1,128)}, f32[1,3,3,1,128]{4,3,2,1,0:T(1,128)}, u32[]{:S(2)}, u32[]{:S(2)}) collective-permute-start(f32[1,3,3,1,128]{4,3,2,1,0:T(1,128)} %get-tuple-element.39), channel_id=1, source_target_pairs={{0,1},{1,2},{2,3},{4,5},{5,6},{6,7},{8,9},{9,10},{10,11},{12,13},{... | collective-permute-start | bytes 13832 | tf_op jit(solution)/shard_map/ppermute | solution.py:31
  86.8 6.4 %collective-permute-start.17 = (f32[1,3,3,1,128]{4,3,2,1,0:T(1,128)}, f32[1,3,3,1,128]{4,3,2,1,0:T(1,128)}, u32[]{:S(2)}, u32[]{:S(2)}) collective-permute-start(f32[1,3,3,1,128]{4,3,2,1,0:T(1,128)} %get-tuple-element.40), channel_id=1, source_target_pairs={{1,0},{2,1},{3,2},{5,4},{6,5},{7,6},{9,8},{10,9},{11,10},{13,12},{... | collective-permute-start | bytes 13832 | tf_op jit(solution)/shard_map/ppermute | solution.py:33
  96.7 2.2 copy-start.6
  96.7 2.2 copy-start.18
  96.7 2.2 copy-start.23
  152.6 21.2 %copy-start.8 = (f32[1,2,128]{2,1,0:T(2,128)}, f32[1,2,128]{2,1,0:T(2,128)S(1)}, u32[]{:S(2)}) copy-start(f32[1,2,128]{2,1,0:T(2,128)S(1)} %bitcast_divide_fusion.1) | copy-start | bytes 3076
  152.6 5.8 %collective-permute-start.19 = (f32[1,1,1,2,128]{4,3,2,1,0:T(2,128)S(1)}, f32[1,1,1,2,128]{4,3,2,1,0:T(2,128)S(1)}, u32[]{:S(2)}, u32[]{:S(2)}) collective-permute-start(f32[1,1,1,2,128]{4,3,2,1,0:T(2,128)S(1)} %bitcast.148), channel_id=1, source_target_pairs={{8,0},{16,8},{24,16},{9,1},{17,9},{25,17},{10,2},{18,10},{26,18},{... | collective-permute-start | bytes 3080 | tf_op jit(solution)/shard_map/ppermute | solution.py:33
  153.9 5.8 %collective-permute-start.18 = (f32[1,1,1,2,128]{4,3,2,1,0:T(2,128)S(1)}, f32[1,1,1,2,128]{4,3,2,1,0:T(2,128)S(1)}, u32[]{:S(2)}, u32[]{:S(2)}) collective-permute-start(f32[1,1,1,2,128]{4,3,2,1,0:T(2,128)S(1)} %bitcast.149), channel_id=1, source_target_pairs={{0,8},{8,16},{16,24},{1,9},{9,17},{17,25},{2,10},{10,18},{18,26},{... | collective-permute-start | bytes 3080 | tf_op jit(solution)/shard_map/ppermute | solution.py:31
  159.7 5.8 %collective-permute-start.21 = (f32[1,3,1,2,128]{4,3,2,1,0:T(2,128)S(1)}, f32[1,3,1,2,128]{4,3,2,1,0:T(2,128)S(1)}, u32[]{:S(2)}, u32[]{:S(2)}) collective-permute-start(f32[1,3,1,2,128]{4,3,2,1,0:T(2,128)S(1)} %pad_maximum_fusion.21), channel_id=1, source_target_pairs={{4,0},{5,1},{6,2},{7,3},{12,8},{13,9},{14,10},{15,11},{20,16},{21,... | collective-permute-start | bytes 9224 | tf_op jit(solution)/shard_map/ppermute | solution.py:33
  161.0 5.9 %collective-permute-start.20 = (f32[1,3,1,2,128]{4,3,2,1,0:T(2,128)S(1)}, f32[1,3,1,2,128]{4,3,2,1,0:T(2,128)S(1)}, u32[]{:S(2)}, u32[]{:S(2)}) collective-permute-start(f32[1,3,1,2,128]{4,3,2,1,0:T(2,128)S(1)} %pad_maximum_fusion.21), channel_id=1, source_target_pairs={{0,4},{1,5},{2,6},{3,7},{8,12},{9,13},{10,14},{11,15},{16,20},{17,... | collective-permute-start | bytes 9224 | tf_op jit(solution)/shard_map/ppermute | solution.py:31
  166.8 2.6 collective-permute-start.22
  168.1 5.6 %collective-permute-start.23 = (f32[1,3,3,1,128]{4,3,2,1,0:T(1,128)S(1)}, f32[1,3,3,1,128]{4,3,2,1,0:T(1,128)S(1)}, u32[]{:S(2)}, u32[]{:S(2)}) collective-permute-start(f32[1,3,3,1,128]{4,3,2,1,0:T(1,128)S(1)} %get-tuple-element.36), channel_id=1, source_target_pairs={{1,0},{2,1},{3,2},{5,4},{6,5},{7,6},{9,8},{10,9},{11,10},{13,12},{... | collective-permute-start | bytes 13832 | tf_op jit(solution)/shard_map/ppermute | solution.py:33
  177.0 2.2 copy-start.9
  177.1 2.2 copy-start.26
  236.9 14.3 %copy-start.15 = (f32[1,2,128]{2,1,0:T(2,128)}, f32[1,2,128]{2,1,0:T(2,128)S(1)}, u32[]{:S(2)}) copy-start(f32[1,2,128]{2,1,0:T(2,128)S(1)} %get-tuple-element.12) | copy-start | bytes 3076
  236.9 5.8 %collective-permute-start.25 = (f32[1,1,1,2,128]{4,3,2,1,0:T(2,128)S(1)}, f32[1,1,1,2,128]{4,3,2,1,0:T(2,128)S(1)}, u32[]{:S(2)}, u32[]{:S(2)}) collective-permute-start(f32[1,1,1,2,128]{4,3,2,1,0:T(2,128)S(1)} %bitcast.154), channel_id=1, source_target_pairs={{8,0},{16,8},{24,16},{9,1},{17,9},{25,17},{10,2},{18,10},{26,18},{... | collective-permute-start | bytes 3080 | tf_op jit(solution)/shard_map/ppermute | solution.py:33
  238.2 5.8 %collective-permute-start.24 = (f32[1,1,1,2,128]{4,3,2,1,0:T(2,128)S(1)}, f32[1,1,1,2,128]{4,3,2,1,0:T(2,128)S(1)}, u32[]{:S(2)}, u32[]{:S(2)}) collective-permute-start(f32[1,1,1,2,128]{4,3,2,1,0:T(2,128)S(1)} %bitcast.155), channel_id=1, source_target_pairs={{0,8},{8,16},{16,24},{1,9},{9,17},{17,25},{2,10},{10,18},{18,26},{... | collective-permute-start | bytes 3080 | tf_op jit(solution)/shard_map/ppermute | solution.py:31
  242.8 10.9 %copy-start.32 = (f32[1,1,1,2,128]{4,3,2,1,0:T(2,128)}, f32[1,1,1,2,128]{4,3,2,1,0:T(2,128)S(1)}, u32[]{:S(2)}) copy-start(f32[1,1,1,2,128]{4,3,2,1,0:T(2,128)S(1)} %collective-permute-done.25) | copy-start | bytes 3076
  244.0 9.6 %copy-start.34 = (f32[1,1,1,2,128]{4,3,2,1,0:T(2,128)}, f32[1,1,1,2,128]{4,3,2,1,0:T(2,128)S(1)}, u32[]{:S(2)}) copy-start(f32[1,1,1,2,128]{4,3,2,1,0:T(2,128)S(1)} %collective-permute-done.24) | copy-start | bytes 3076
  244.0 5.8 %collective-permute-start.27 = (f32[1,3,1,2,128]{4,3,2,1,0:T(2,128)S(1)}, f32[1,3,1,2,128]{4,3,2,1,0:T(2,128)S(1)}, u32[]{:S(2)}, u32[]{:S(2)}) collective-permute-start(f32[1,3,1,2,128]{4,3,2,1,0:T(2,128)S(1)} %pad_maximum_fusion.22), channel_id=1, source_target_pairs={{4,0},{5,1},{6,2},{7,3},{12,8},{13,9},{14,10},{15,11},{20,16},{21,... | collective-permute-start | bytes 9224 | tf_op jit(solution)/shard_map/ppermute | solution.py:33
  245.3 5.9 %collective-permute-start.26 = (f32[1,3,1,2,128]{4,3,2,1,0:T(2,128)S(1)}, f32[1,3,1,2,128]{4,3,2,1,0:T(2,128)S(1)}, u32[]{:S(2)}, u32[]{:S(2)}) collective-permute-start(f32[1,3,1,2,128]{4,3,2,1,0:T(2,128)S(1)} %pad_maximum_fusion.22), channel_id=1, source_target_pairs={{0,4},{1,5},{2,6},{3,7},{8,12},{9,13},{10,14},{11,15},{16,20},{17,... | collective-permute-start | bytes 9224 | tf_op jit(solution)/shard_map/ppermute | solution.py:31
  249.9 1.9 copy-start.27
  251.8 8.7 %collective-permute-start.28 = (f32[1,3,3,1,128]{4,3,2,1,0:T(1,128)}, f32[1,3,3,1,128]{4,3,2,1,0:T(1,128)}, u32[]{:S(2)}, u32[]{:S(2)}) collective-permute-start(f32[1,3,3,1,128]{4,3,2,1,0:T(1,128)} %get-tuple-element.31), channel_id=1, source_target_pairs={{0,1},{1,2},{2,3},{4,5},{5,6},{6,7},{8,9},{9,10},{10,11},{12,13},{... | collective-permute-start | bytes 13832 | tf_op jit(solution)/shard_map/ppermute | solution.py:31
  253.7 6.8 %collective-permute-start.29 = (f32[1,3,3,1,128]{4,3,2,1,0:T(1,128)}, f32[1,3,3,1,128]{4,3,2,1,0:T(1,128)}, u32[]{:S(2)}, u32[]{:S(2)}) collective-permute-start(f32[1,3,3,1,128]{4,3,2,1,0:T(1,128)} %get-tuple-element.32), channel_id=1, source_target_pairs={{1,0},{2,1},{3,2},{5,4},{6,5},{7,6},{9,8},{10,9},{11,10},{13,12},{... | collective-permute-start | bytes 13832 | tf_op jit(solution)/shard_map/ppermute | solution.py:33
  267.3 2.3 copy-start.16
  267.3 2.3 copy-start.36
  269.5 59.2 %copy-start.4 = (f32[3,2,128]{2,1,0:T(2,128)S(1)}, f32[3,2,128]{2,1,0:T(2,128)}, u32[]{:S(2)}) copy-start(f32[3,2,128]{2,1,0:T(2,128)} %copy-done.3) | copy-start | bytes 9220
  269.5 59.2 %copy-start.7 = (f32[2,128]{1,0:T(2,128)S(1)}, f32[2,128]{1,0:T(2,128)}, u32[]{:S(2)}) copy-start(f32[2,128]{1,0:T(2,128)} %copy-done.5) | copy-start | bytes 3076
  269.5 59.2 %copy-start.11 = (f32[3,1,1,2,128]{4,3,2,1,0:T(2,128)S(1)}, f32[3,1,1,2,128]{4,3,2,1,0:T(2,128)}, u32[]{:S(2)}) copy-start(f32[3,1,1,2,128]{4,3,2,1,0:T(2,128)} %param.4) | copy-start | bytes 9220
  269.5 59.2 %copy-start.14 = (f32[6,2,128]{2,1,0:T(2,128)S(1)}, f32[6,2,128]{2,1,0:T(2,128)}, u32[]{:S(2)}) copy-start(f32[6,2,128]{2,1,0:T(2,128)} %copy-done.12) | copy-start | bytes 18436
  269.6 59.2 %copy-start.25 = (f32[3,2]{1,0:T(4,128)S(1)}, f32[3,2]{1,0:T(4,128)}, u32[]{:S(2)}) copy-start(f32[3,2]{1,0:T(4,128)} %copy.31) | copy-start | bytes 76
  323.7 5.8 %copy-start.37 = (f32[1,2,128]{2,1,0:T(2,128)}, f32[1,2,128]{2,1,0:T(2,128)S(1)}, u32[]{:S(2)}) copy-start(f32[1,2,128]{2,1,0:T(2,128)S(1)} %multiply_add_fusion.1) | copy-start | bytes 3076
  (5 other events, 7.4 us)
